TPU v7x, 32 devices: a whole 2x2x4 slice. The times are simulated.
32 devices in a mesh: dp: 4 (over y, x), expert: 8 (over z, core).
Axes of the slice: x: 2, y: 2, z: 4, core: 2. Of those that a mesh axis runs over, the one named last changes fastest.
Arguments:
- hidden: bfloat16 [32, 2048], P(('dp', 'expert')), may hold values from -6 to 6
- attn_gain: float32 [2048], replicated, may hold values from 0.25 to 1.75
- query_weight: bfloat16 [3072, 2048], P('expert'), may hold values from -0.125 to 0.125
- latent_down: bfloat16 [2048, 576], replicated, may hold values from -0.125 to 0.125
- latent_up: bfloat16 [512, 4096], P(None, 'expert'), may hold values from -0.25 to 0.25
- out_weight: bfloat16 [2048, 2048], P('expert'), may hold values from -0.125 to 0.125
- latent_pool: bfloat16 [128, 32, 576], P('dp'), may hold values from -1000 to 1000
- page_table: int32 [32, 16], replicated, may hold values from -1 to 127, as said below
- page_counts: int32 [32], replicated, may hold values from 1 to 16, as said below
- ffn_gain: float32 [2048], replicated, may hold values from 0.25 to 1.75
- expert_ids: int32 [32, 6], replicated, may hold values from 0 to 23, all different within a row; in each aligned block of 32 rows (0 to 31, 32 to 63, ...) at most 16 rows name the same one
- expert_gates: float32 [32, 6], replicated, may hold values from 0.05 to 0.6
- old_place: int32 [8, 4], replicated, may hold values from 0 to 23, as said below
- new_place: int32 [8, 4], replicated, may hold values from 0 to 23, as said below
- expert_gate_up: bfloat16 [32, 2, 1408, 2048], P('expert', None, None, 'dp'), as said below
- expert_down: bfloat16 [32, 1408, 2048], P('expert', None, 'dp'), as said below
- shared_gate_up: bfloat16 [2, 2816, 2048], P(None, None, 'dp'), may hold values from -0.125 to 0.125
- shared_down: bfloat16 [2816, 2048], P(None, 'dp'), may hold values from -0.109375 to 0.109375
Outputs:
- layer_out: bfloat16 [32, 2048], P(('dp', 'expert'))
- moved_gate_up: bfloat16 [32, 2, 1408, 2048], P('expert', None, None, 'dp')
- moved_down: bfloat16 [32, 1408, 2048], P('expert', None, 'dp')
Inputs may be any that keep to these rules, and one draw needn't show every extreme that they name: `page_counts`: each request's count of cached pages; exactly one request has 16. `page_table`: row t names page_counts[t] pages of the pool, no page named twice in the table; its other entries are -1. Page p lies on dp index p // 32. `expert_ids`: no expert is named by more than 16 tokens in all; some expert by exactly 16. `old_place`: row i holds the experts of the slots on expert index i, slot s of row i being global slot i * 4 + s; every expert is held by one slot or more. `new_place`: equal to old_place except in exactly one slot of each row, which names another expert. `expert_gate_up`: slots that hold the same expert under old_place hold equal weights. `expert_down`: slots that hold the same expert under old_place hold equal weights.
All inputs are finite; a program needn't handle non-finite values.
Results may differ from a plain program's by a relative error of at most 0.02.
Values may be sent and summed in bfloat16 or wider, within the bound.
No kernel may reach another device: no remote copies, remote signals or barrier semaphores. Data moves between devices by JAX's collectives and lax.ppermute only.
A program may use at most 128 MiB of HBM per device.

v0:
```python
import math
import jax
import jax.numpy as jnp
from jax import lax
from jax.sharding import PartitionSpec as P

NOPE = 128
ROPE = 64
VHEAD = 128
LATENT = 512
EXP_DEV = 3
PAGE = 32
EPSILON = 1e-06
ROPE_BASE = 50000.0
MASKED_SCORE = -1e30
HIGHEST = lax.Precision.HIGHEST


def rms_plain(values):
    mean_square = jnp.mean(values * values, axis=-1, keepdims=True)
    return values * lax.rsqrt(mean_square + EPSILON)


def rms_norm(values, norm_gain):
    return rms_plain(values) * norm_gain


def rotary(values, position):
    half_width = values.shape[-1] // 2
    exponent = jnp.arange(half_width).astype(jnp.float32) * (2.0 / values.shape[-1])
    frequency = jnp.exp(-exponent * math.log(ROPE_BASE))
    angles = position[..., None] * frequency
    cosine = jnp.cos(angles)
    sine_part = jnp.sin(angles)
    first_half = values[..., :half_width]
    second = values[..., half_width:]
    return jnp.concatenate(
        [first_half * cosine - second * sine_part, second * cosine + first_half * sine_part],
        axis=-1,
    )


def gather_rows(rows):
    by_expert = lax.all_gather(rows, "expert", axis=0, tiled=True)
    return lax.all_gather(by_expert, "dp", axis=0, tiled=True)


def spread_slots(gate_up, down, picks, ex_count):
    chosen = jnp.concatenate([gate_up[picks], down[picks][:, None]], axis=1)
    count, parts, ff_width, col_width = chosen.shape
    pieces = chosen.reshape(count, parts, ex_count, ff_width // ex_count, col_width)
    spread = lax.all_to_all(pieces, "expert", split_axis=2, concat_axis=0, tiled=True)
    return spread.reshape(ex_count * count, parts, ff_width // ex_count, col_width)


def migrate(expert_gate_up, expert_down, old_place, new_place, ex_index):
    rows, slots_local = old_place.shape
    slots = rows * slots_local
    ex_count = rows
    ff_width = expert_gate_up.shape[2]
    changed = old_place != new_place
    moved_slot = jnp.argmax(changed, axis=1)
    wanted = jnp.take_along_axis(new_place, moved_slot[:, None], axis=1)[:, 0]
    hit = old_place.reshape(-1)[None, :] == wanted[:, None]
    first = jnp.argmax(hit, axis=1).astype(jnp.int32)
    last = (slots - 1 - jnp.argmax(hit[:, ::-1], axis=1)).astype(jnp.int32)
    slot_ids = jnp.arange(slots, dtype=jnp.int32)

    def needed_of(src):
        needed = jnp.any(src[:, None] == slot_ids[None, :], axis=0).reshape(rows, slots_local)
        return (needed, jnp.max(jnp.sum(needed.astype(jnp.int32), axis=1)))

    need_first, load_first = needed_of(first)
    need_last, load_last = needed_of(last)
    use_last = load_last < load_first
    source = jnp.where(use_last, last, first)
    needed = jnp.where(use_last, need_last, need_first)
    load = jnp.minimum(load_first, load_last)
    rank = jnp.cumsum(needed.astype(jnp.int32), axis=1) - 1
    local_ids = jnp.arange(slots_local, dtype=jnp.int32)
    picks = jnp.stack(
        [jnp.argmax(needed & (rank == k), axis=1).astype(jnp.int32) for k in range(slots_local)],
        axis=1,
    )
    my_picks = picks[ex_index]
    src_dev = source // slots_local
    src_rank = rank.reshape(-1)[source]
    fast = min(2, slots_local)
    spread_a = spread_slots(expert_gate_up, expert_down, my_picks[:fast], ex_count)
    out_a = spread_a[src_dev * fast + jnp.minimum(src_rank, fast - 1)]
    if slots_local > fast:
        rest = slots_local - fast

        def extra():
            spread_b = spread_slots(expert_gate_up, expert_down, my_picks[fast:], ex_count)
            return spread_b[src_dev * rest + jnp.clip(src_rank - fast, 0, rest - 1)]

        out_b = lax.cond(load > fast, extra, lambda: jnp.zeros_like(out_a))
        out_a = jnp.where((src_rank < fast)[:, None, None, None], out_a, out_b)
    arrived = lax.all_to_all(out_a, "expert", split_axis=0, concat_axis=2, tiled=True)
    is_moved = local_ids == moved_slot[ex_index]
    moved_gate_up = jnp.where(is_moved[:, None, None, None], arrived[:, :2], expert_gate_up)
    moved_down = jnp.where(is_moved[:, None, None], arrived[:, 2], expert_down)
    return (moved_gate_up, moved_down)


def local(
    hidden,
    attn_gain,
    query_weight,
    latent_down,
    latent_up,
    out_weight,
    latent_pool,
    page_table,
    page_counts,
    ffn_gain,
    expert_ids,
    expert_gates,
    old_place,
    new_place,
    expert_gate_up,
    expert_down,
    shared_gate_up,
    shared_down,
):
    dp_count = lax.axis_size("dp")
    ex_count = lax.axis_size("expert")
    dp_index = lax.axis_index("dp")
    ex_index = lax.axis_index("expert")
    req_local = hidden.shape[0]
    group_rows = req_local * ex_count
    requests = page_counts.shape[0]
    head_local = query_weight.shape[0] // (NOPE + ROPE)
    score_scale = (NOPE + ROPE) ** (-0.5)
    group_start = dp_index * group_rows
    everyone = gather_rows(hidden)
    normed = rms_norm(everyone.astype(jnp.float32), attn_gain).astype(jnp.bfloat16)
    queries = jnp.einsum(
        "td,qd->tq", normed, query_weight, preferred_element_type=jnp.float32
    ).reshape(requests, head_local, NOPE + ROPE)
    position = (page_counts * PAGE).astype(jnp.float32)
    query_rope = rotary(queries[..., NOPE:], position[:, None]).astype(jnp.bfloat16)
    up_table = latent_up.reshape(LATENT, head_local, NOPE + VHEAD)
    query_latent = jnp.einsum(
        "thn,lhn->thl",
        queries[..., :NOPE],
        up_table[..., :NOPE].astype(jnp.float32),
        precision=HIGHEST,
    ).astype(jnp.bfloat16)
    pages_local = latent_pool.shape[0]
    pool_total = pages_local * dp_count
    flat_pages = page_table.reshape(-1)
    flat_owner = jnp.repeat(jnp.arange(requests, dtype=jnp.int32), page_table.shape[1])
    target = jnp.where(flat_pages >= 0, flat_pages, pool_total)
    owner_all = jnp.full((pool_total,), -1, jnp.int32).at[target].set(flat_owner, mode="drop")
    page_owner = lax.dynamic_slice_in_dim(owner_all, dp_index * pages_local, pages_local)
    page_used = page_owner >= 0
    owner_safe = jnp.maximum(page_owner, 0)
    page_latent = latent_pool[..., :LATENT]
    page_rope = latent_pool[..., LATENT:]
    scores = jnp.einsum(
        "phl,pkl->phk", query_latent[owner_safe], page_latent, preferred_element_type=jnp.float32
    )
    scores = (
        scores
        + jnp.einsum(
            "phr,pkr->phk", query_rope[owner_safe], page_rope, preferred_element_type=jnp.float32
        )
    ) * score_scale
    raw_max = jnp.max(scores, axis=2)
    weights = jnp.exp(scores - raw_max[..., None])
    page_total = jnp.sum(weights, axis=2)
    page_mix = jnp.einsum(
        "phk,pkl->phl",
        weights.astype(jnp.bfloat16),
        page_latent,
        preferred_element_type=jnp.float32,
    )
    page_max = jnp.where(page_used[:, None], raw_max, MASKED_SCORE)
    member = page_owner[None, :] == jnp.arange(requests, dtype=jnp.int32)[:, None]
    req_max = jnp.max(jnp.where(member[:, :, None], page_max[None], MASKED_SCORE), axis=1)
    rescale = jnp.where(page_used[:, None], jnp.exp(page_max - req_max[owner_safe]), 0.0)
    member_float = member.astype(jnp.float32)
    req_total = jnp.dot(member_float, page_total * rescale, precision=HIGHEST)
    req_mix = jnp.einsum(
        "rp,phl->rhl", member_float, page_mix * rescale[..., None], precision=HIGHEST
    )
    packed = jnp.concatenate([req_mix, req_max[..., None], req_total[..., None]], axis=-1)
    gathered = lax.all_gather(packed, "dp", axis=0, tiled=False)
    gathered = lax.dynamic_slice_in_dim(gathered, group_start, group_rows, 1)
    each_max = gathered[..., LATENT]
    part_max = jnp.max(each_max, axis=0)
    each_weight = jnp.exp(each_max - part_max[None])
    part_total = jnp.sum(gathered[..., LATENT + 1] * each_weight, axis=0)
    part_mix = jnp.sum(gathered[..., :LATENT] * each_weight[..., None], axis=0)
    own_normed = lax.dynamic_slice_in_dim(normed, group_start, group_rows, 0)
    own_position = lax.dynamic_slice_in_dim(position, group_start, group_rows, 0)
    fresh_latent = jnp.dot(own_normed, latent_down, preferred_element_type=jnp.float32)
    new_latent = rms_plain(fresh_latent[:, :LATENT]).astype(jnp.bfloat16)
    new_rope = rotary(fresh_latent[:, LATENT:], own_position).astype(jnp.bfloat16)
    own_query = lax.dynamic_slice_in_dim(query_latent, group_start, group_rows, 0)
    own_rope_query = lax.dynamic_slice_in_dim(query_rope, group_start, group_rows, 0)
    own_score = jnp.einsum("thl,tl->th", own_query, new_latent, preferred_element_type=jnp.float32)
    own_score = (
        own_score
        + jnp.einsum("thr,tr->th", own_rope_query, new_rope, preferred_element_type=jnp.float32)
    ) * score_scale
    highest = jnp.maximum(part_max, own_score)
    kept_part = jnp.exp(part_max - highest)
    own_weight = jnp.exp(own_score - highest)
    denominator = part_total * kept_part + own_weight
    numerator = (
        part_mix * kept_part[..., None]
        + own_weight[..., None] * new_latent.astype(jnp.float32)[:, None, :]
    )
    attended = (numerator / denominator[..., None]).astype(jnp.bfloat16)
    heads_out = jnp.einsum(
        "thl,lhv->thv", attended, up_table[..., NOPE:], preferred_element_type=jnp.float32
    )
    heads_out = heads_out.astype(jnp.bfloat16).reshape(group_rows, head_local * VHEAD)
    partial_value = jnp.dot(heads_out, out_weight, preferred_element_type=jnp.float32)
    attn_out = lax.psum_scatter(partial_value, "expert", scatter_dimension=0, tiled=True)
    residual = hidden.astype(jnp.float32) + attn_out
    normed_ffn = rms_norm(residual, ffn_gain).astype(jnp.bfloat16)
    slots_local = expert_gate_up.shape[0]
    ff_width = expert_gate_up.shape[2]
    col_width = expert_gate_up.shape[3]
    every_row = gather_rows(normed_ffn)
    my_columns = lax.dynamic_slice_in_dim(every_row, dp_index * col_width, col_width, 1)
    by_group = my_columns.reshape(dp_count, ex_count, req_local, col_width).transpose(1, 0, 2, 3)
    ffn_rows = by_group.reshape(requests, col_width)
    column_rows = lax.dynamic_index_in_dim(by_group, ex_index, 0, keepdims=False).reshape(
        dp_count * req_local, col_width
    )
    top_count = expert_ids.shape[1]
    experts_count = EXP_DEV * ex_count
    ids_order = (
        expert_ids.reshape(dp_count, ex_count, req_local, top_count)
        .transpose(1, 0, 2, 3)
        .reshape(requests, top_count)
    )
    gates_order = (
        expert_gates.reshape(dp_count, ex_count, req_local, top_count)
        .transpose(1, 0, 2, 3)
        .reshape(requests, top_count)
    )
    old_flat = old_place.reshape(-1)
    holds_map = old_flat[None, :] == jnp.arange(experts_count, dtype=jnp.int32)[:, None]
    holder = jnp.argmax(holds_map, axis=1)
    slot_of = holder[ids_order.reshape(-1)]
    capacity = 2 * requests * top_count // experts_count
    local_slot = slot_of - ex_index * slots_local
    slot_hot = local_slot[:, None] == jnp.arange(slots_local, dtype=jnp.int32)[None, :]
    slot_rank = jnp.cumsum(slot_hot.astype(jnp.int32), axis=0) - 1
    position_in = jnp.where(slot_hot, slot_rank, capacity)
    route_hot = (
        position_in[:, :, None] == jnp.arange(capacity, dtype=jnp.int32)[None, None, :]
    ).astype(jnp.float32)
    route_hot = route_hot.reshape(requests, top_count, slots_local, capacity)
    dispatch = jnp.sum(route_hot, axis=1).astype(jnp.bfloat16)
    combine = jnp.sum(route_hot * gates_order[:, :, None, None], axis=1)
    slot_inputs = jnp.einsum(
        "tsc,td->scd", dispatch, ffn_rows, preferred_element_type=jnp.float32
    ).astype(jnp.bfloat16)
    routed_part = jnp.einsum(
        "scd,sgfd->sgcf", slot_inputs, expert_gate_up, preferred_element_type=jnp.float32
    )
    shared_part = jnp.einsum(
        "td,gfd->gtf", column_rows, shared_gate_up, preferred_element_type=jnp.float32
    )
    routed_sum, shared_sum = lax.psum((routed_part, shared_part), "dp")
    activated = (jax.nn.silu(routed_sum[:, 0]) * routed_sum[:, 1]).astype(jnp.bfloat16)
    slot_out = jnp.einsum(
        "scf,sfd->scd", activated, expert_down, preferred_element_type=jnp.float32
    )
    routed = jnp.einsum("tsc,scd->td", combine, slot_out, precision=HIGHEST)
    shared_act = (jax.nn.silu(shared_sum[0]) * shared_sum[1]).astype(jnp.bfloat16)
    shared_term = jnp.dot(shared_act, shared_down, preferred_element_type=jnp.float32)
    moe_rows = lax.psum_scatter(routed, "expert", scatter_dimension=0, tiled=True)
    moe_part = lax.all_to_all(moe_rows + shared_term, "dp", split_axis=0, concat_axis=1, tiled=True)
    layer_out = (residual + moe_part).astype(jnp.bfloat16)
    moved_gate_up, moved_down = migrate(expert_gate_up, expert_down, old_place, new_place, ex_index)
    return (layer_out, moved_gate_up, moved_down)


def solution(mesh):
    in_specs = (
        P(("dp", "expert"), None),
        P(),
        P("expert", None),
        P(),
        P(None, "expert"),
        P("expert", None),
        P("dp", None, None),
        P(),
        P(),
        P(),
        P(),
        P(),
        P(),
        P(),
        P("expert", None, None, "dp"),
        P("expert", None, "dp"),
        P(None, None, "dp"),
        P(None, "dp"),
    )
    out_specs = (P(("dp", "expert"), None), P("expert", None, None, "dp"), P("expert", None, "dp"))
    return jax.shard_map(local, mesh=mesh, in_specs=in_specs, out_specs=out_specs, check_vma=False)
```

profile of v0, /device:TPU:0, one launch (start us, length us, event | category | flops | bytes accessed | tf_op | source)
XLA Modules:
  0.0 691.7 jit_solution(8807751896408755276)
XLA Ops:
  18.1 5.9 mini-gather-slice.2
  24.0 5.2 mini-gather-slice.3
  30.6 5.2 gather_fusion.11
  35.8 4.7 gather_fusion.12
  40.5 5.0 gather_fusion.8
  45.5 5.6 pad_maximum_fusion.3
  51.1 7.7 %pad_maximum_fusion.2 = bf16[2,3,8,176,512]{4,3,2,1,0:T(8,128)(2,1)} fusion(bf16[2,1,8,176,512]{4,3,2,1,0:T(8,128)(2,1)} %bitcast.229, bf16[2,2,8,176,512]{4,3,2,1,0:T(8,128)(2,1)} %bitcast.225), kind=kLoop, calls=%fused_computation.22 | loop fusion | flops 4325376 | bytes 17301504 | tf_op jit(solution)/shard_map/concatenate | solution.py:49
  58.8 7.6 %copy.166 = bf16[2,3,8,176,512]{4,3,1,0,2:T(8,128)(2,1)} copy(bf16[2,3,8,176,512]{4,3,2,1,0:T(8,128)(2,1)} %pad_maximum_fusion.2) | data formatting | bytes 17301504 | tf_op jit(solution)/shard_map/concatenate | solution.py:49
  68.7 2.5 conditional.1
  71.3 6.5 all-to-all-start.2
  77.8 195.6 %all-gather.1 = bf16[8,1,2048]{2,1,0:T(2,128)(2,1)S(1)} all-gather(bf16[1,1,2048]{2,1,0:T(2,128)(2,1)S(1)} %bitcast.240), channel_id=1, replica_groups=mesh['dp'=4,'expert'=8] {'expert'}, dimensions={0}, use_global_device_ids=true | all-gather | bytes 36864 | tf_op jit(solution)/shard_map/all_gather | solution.py:44
  273.4 8.5 %all_gather.19 = bf16[32,2048]{1,0:T(8,128)(2,1)S(1)} all-gather(bf16[8,2048]{1,0:T(8,128)(2,1)S(1)} %bitcast.236), channel_id=1, replica_groups=mesh['dp'=4,'expert'=8] {'dp'}, dimensions={0}, use_global_device_ids=true | all-gather | bytes 163840 | tf_op jit(solution)/shard_map/all_gather | solution.py:45
  289.1 2.6 scatter_custom_fusion
  320.0 11.4 %all-gather = f32[128,2,514]{2,0,1:T(8,128)S(1)} all-gather(f32[32,2,514]{2,0,1:T(8,128)S(1)} %pad_maximum_fusion.4), channel_id=2, replica_groups=mesh['dp'=4,'expert'=8] {'dp'}, dimensions={0}, use_global_device_ids=true | all-gather | bytes 657920 | tf_op jit(solution)/shard_map/all_gather | solution.py:190
  345.4 3.0 multiply_reduce_fusion
  354.8 4.5 compare_select_fusion.5
  359.4 10.5 %select_subtract_fusion = s32[192]{0:T(256)S(1)} fusion(pred[192]{0:T(512)(128)(4,1)S(1)} %get-tuple-element.86, pred[192]{0:T(512)(128)(4,1)S(1)} %get-tuple-element.85, pred[192]{0:T(512)(128)(4,1)S(1)} %get-tuple-element.84, pred[192]{0:T(512)(128)(4,1)S(1)} %get-tuple-element.83, pred[192]{0:T(512)(128)(4,1)S(1)} %get-tuple-element.82, ...), kind=kLoop, calls=%fused_computation.212 | loop fusion | flops 3456 | bytes 4872 | tf_op jit(solution)/shard_map/sub | solution.py:253
  372.7 32.9 %all-reduce.8.cloned.1.call-done = f32[8,2048]{1,0:T(8,128)} async-done(((f32[8,2048]{1,0:T(8,128)}), f32[8,2048]{1,0:T(8,128)}) %all-reduce.8.cloned.1.call-update) | async-done | bytes 65552
  408.4 14.0 %all-gather.2 = bf16[8,1,2048]{2,1,0:T(2,128)(2,1)S(1)} all-gather(bf16[1,1,2048]{2,1,0:T(2,128)(2,1)S(1)} %convert_bitcast_fusion), channel_id=1, replica_groups=mesh['dp'=4,'expert'=8] {'expert'}, dimensions={0}, use_global_device_ids=true | all-gather | bytes 36864 | tf_op jit(solution)/shard_map/all_gather | solution.py:44
  422.4 8.4 %all_gather.23 = bf16[32,2048]{1,0:T(8,128)(2,1)S(1)} all-gather(bf16[8,2048]{1,0:T(8,128)(2,1)S(1)} %bitcast.237), channel_id=1, replica_groups=mesh['dp'=4,'expert'=8] {'dp'}, dimensions={0}, use_global_device_ids=true | all-gather | bytes 163840 | tf_op jit(solution)/shard_map/all_gather | solution.py:45
  430.9 4.9 convolution_bitcast_fusion
  435.8 6.9 convolution_bitcast_fusion.1
  443.4 46.9 %all-reduce.12.cloned.1.call-done = (f32[2,4,2816]{2,1,0:T(4,128)}, f32[4,2,16,1408]{3,2,1,0:T(8,128)}) async-done(((f32[2,4,2816]{2,1,0:T(4,128)}, f32[4,2,16,1408]{3,2,1,0:T(8,128)}), (f32[2,4,2816]{2,1,0:T(4,128)}, f32[4,2,16,1408]{3,2,1,0:T(8,128)})) %all-reduce.12.cloned.1.call-update) | async-done | bytes 811024 | tf_op jit(solution)/shard_map/psum | solution.py:272
  490.3 3.8 fusion.18
  495.6 53.2 %all-reduce.10.cloned.1.call-done = f32[32,512]{1,0:T(8,128)} async-done(((f32[32,512]{1,0:T(8,128)}), f32[32,512]{1,0:T(8,128)}) %all-reduce.10.cloned.1.call-update) | async-done | bytes 65552
  550.6 3.6 all-to-all-start.1
  554.3 6.3 gather_fusion.9
  560.6 6.1 broadcast_select_fusion.2
  566.7 4.6 all-to-all-start.3
  573.1 95.0 %all-to-all-done.3 = bf16[8,3,176,512]{3,2,1,0:T(8,128)(2,1)} async-done(((bf16[8,3,176,512]{3,2,1,0:T(8,128)(2,1)}), bf16[8,3,176,512]{3,2,1,0:T(8,128)(2,1)}, u32[]{:S(2)}, u32[]{:S(2)}) %all-to-all-start.3) | async-done | bytes 4325408 | tf_op jit(solution)/shard_map/all_to_all | solution.py:100
  670.9 11.0 %broadcast_select_fusion = bf16[4,2,1408,512]{3,2,1,0:T(8,128)(2,1)} fusion(bf16[4,2,1408,512]{3,2,1,0:T(8,128)(2,1)} %param.34, pred[4]{0:T(512)(128)(4,1)S(1)} %iota_compare_fusion.9, bf16[2,1408,512]{2,1,0:T(8,128)(2,1)S(1)} %slice_bitcast_fusion), kind=kLoop, calls=%fused_computation.21 | loop fusion | flops 5767168 | bytes 25952260 | tf_op jit(solution)/shard_map/jit(_where)/select_n | solution.py:102
  681.9 3.2 broadcast_select_fusion.1
  (221 shorter events, 83.6 us)
Async XLA Ops:
  7.2 541.6 %copy-start = (bf16[2816,512]{1,0:T(8,128)(2,1)S(1)}, bf16[2816,512]{1,0:T(8,128)(2,1)}, u32[]{:S(2)}) copy-start(bf16[2816,512]{1,0:T(8,128)(2,1)} %param.37) | copy-start | bytes 8650756
  9.3 2.3 copy-start.26
  10.8 1.6 copy-start.19
  71.3 6.5 copy-start.10
  71.3 210.8 %copy-start.16 = (f32[2048]{0:T(1024)S(1)}, f32[2048]{0:T(1024)}, u32[]{:S(2)}) copy-start(f32[2048]{0:T(1024)} %param.21) | copy-start | bytes 24580
  71.3 213.0 %copy-start.17 = (s32[32,16]{0,1:T(8,128)S(1)}, s32[32,16]{0,1:T(8,128)}, u32[]{:S(2)}) copy-start(s32[32,16]{0,1:T(8,128)} %param.27) | copy-start | bytes 6148
  71.3 479.3 %all-to-all-start.2 = ((bf16[2,3,8,176,512]{4,3,1,0,2:T(8,128)(2,1)}), bf16[2,3,8,176,512]{4,3,1,0,2:T(8,128)(2,1)}, u32[]{:S(2)}, u32[]{:S(2)}) async-start(bf16[2,3,8,176,512]{4,3,1,0,2:T(8,128)(2,1)} %copy.166), calls=%async_computation.2 | async-start | bytes 17301504 | tf_op jit(solution)/shard_map/all_to_all | solution.py:52
  77.7 327.9 %all-reduce.8.cloned.1.call-start = ((), (), s32[]{:S(2)}) async-start(), calls=%async_computation.4 | async-start | bytes 131072
  286.8 55.8 %copy-start.1 = (bf16[512,512]{0,1:T(8,128)(2,1)}, bf16[512,512]{0,1:T(8,128)(2,1)S(1)}, u32[]{:S(2)}) copy-start(bf16[512,512]{0,1:T(8,128)(2,1)S(1)} %copy.145) | copy-start | bytes 1572868
  287.8 0.6 copy-start.4
  291.7 2.0 copy-start.23
  302.9 3.3 copy-start.6
  331.3 0.8 copy-start.2
  332.9 12.5 %copy-start.13 = (f32[8,2]{0,1:T(2,128)}, f32[8,2]{0,1:T(2,128)S(1)}, u32[]{:S(2)}) copy-start(f32[8,2]{0,1:T(2,128)S(1)} %get-tuple-element.98) | copy-start | bytes 196
  333.8 11.6 %copy-start.9 = (f32[4,8,2,1]{1,0,3,2:T(4,128)}, f32[4,8,2,1]{1,0,3,2:T(4,128)S(1)}, u32[]{:S(2)}) copy-start(f32[4,8,2,1]{1,0,3,2:T(4,128)S(1)} %copy.182) | copy-start | bytes 772
  337.6 0.6 copy-start.5
  338.2 10.3 %copy-start.14 = (f32[4,8,2,1]{1,0,3,2:T(4,128)S(1)}, f32[4,8,2,1]{1,0,3,2:T(4,128)}, u32[]{:S(2)}) copy-start(f32[4,8,2,1]{1,0,3,2:T(4,128)} %copy.183) | copy-start | bytes 772
  338.2 14.2 %copy-start.21 = (s32[32,6]{0,1:T(8,128)S(1)}, s32[32,6]{0,1:T(8,128)}, u32[]{:S(2)}) copy-start(s32[32,6]{0,1:T(8,128)} %param.30) | copy-start | bytes 2308
  338.2 14.5 %copy-start.20 = (s32[32]{0:T(128)S(1)}, s32[32]{0:T(128)}, u32[]{:S(2)}) copy-start(s32[32]{0:T(128)} %copy-done.19) | copy-start | bytes 388
  338.2 33.5 %copy-start.22 = (f32[32,6]{0,1:T(8,128)S(1)}, f32[32,6]{0,1:T(8,128)}, u32[]{:S(2)}) copy-start(f32[32,6]{0,1:T(8,128)} %param.31) | copy-start | bytes 2308
  338.2 33.8 %copy-start.28 = (u32[32]{0:T(128)S(1)}, u32[32]{0:T(128)}, u32[]{:S(2)}) copy-start(u32[32]{0:T(128)} %constant.206) | copy-start | bytes 388
  338.3 67.3 %copy-start.11 = (bf16[1,2048]{1,0:T(2,128)(2,1)S(1)}, bf16[1,2048]{1,0:T(2,128)(2,1)}, u32[]{:S(2)}) copy-start(bf16[1,2048]{1,0:T(2,128)(2,1)} %param.20) | copy-start | bytes 12292
  338.3 70.1 %copy-start.18 = (f32[2048]{0:T(1024)S(1)}, f32[2048]{0:T(1024)}, u32[]{:S(2)}) copy-start(f32[2048]{0:T(1024)} %param.29) | copy-start | bytes 24580
  352.4 137.9 %all-reduce.12.cloned.1.call-start = ((), (), s32[]{:S(2)}) async-start(), calls=%async_computation.6 | async-start | bytes 1622016 | tf_op jit(solution)/shard_map/psum | solution.py:272
  442.7 106.1 %all-reduce.10.cloned.1.call-start = ((), (), s32[]{:S(2)}) async-start(), calls=%async_computation.5 | async-start | bytes 131072
  490.3 4.7 copy-start.24
  490.3 58.5 %copy-start.12 = (f32[2,4,2816]{2,1,0:T(4,128)S(1)}, f32[2,4,2816]{2,1,0:T(4,128)}, u32[]{:S(2)}) copy-start(f32[2,4,2816]{2,1,0:T(4,128)} %get-tuple-element.87) | copy-start | bytes 270340
  550.6 16.1 %all-to-all-start.1 = ((f32[4,1,512]{2,1,0:T(1,128)}), f32[4,1,512]{2,1,0:T(1,128)S(1)}, u32[]{:S(2)}, u32[]{:S(2)}) async-start(f32[4,1,512]{2,1,0:T(1,128)} %copy.164), calls=%async_computation.1 | async-start | bytes 16384 | tf_op jit(solution)/shard_map/all_to_all | solution.py:281
  566.7 4.6 copy-start.27
  566.7 101.4 %all-to-all-start.3 = ((bf16[8,3,176,512]{3,2,1,0:T(8,128)(2,1)}), bf16[8,3,176,512]{3,2,1,0:T(8,128)(2,1)}, u32[]{:S(2)}, u32[]{:S(2)}) async-start(bf16[8,3,176,512]{3,2,1,0:T(8,128)(2,1)} %broadcast_select_fusion.2), calls=%async_computation.3 | async-start | bytes 8650752 | tf_op jit(solution)/shard_map/all_to_all | solution.py:100
  670.6 11.3 %slice-start = ((s8[5767168]{0:T(1024)(128)(4,1)}), s8[4194304]{0:T(1024)(128)(4,1)S(1)}, s32[]{:S(2)}) async-start(s8[5767168]{0:T(1024)(128)(4,1)} %bitcast.223), calls=%async_computation.7 | async-start | bytes 8388608
  670.9 11.0 %slice-start.1 = ((s8[5767168]{0:T(1024)(128)(4,1)}), s8[1572864]{0:T(1024)(128)(4,1)S(1)}, s32[]{:S(2)}) async-start(s8[5767168]{0:T(1024)(128)(4,1)} %bitcast.223), calls=%async_computation.8 | async-start | bytes 3145728
  (5 other events, 3.0 us)
Sparse Core Ops, SparseCore 0:
  352.5 53.0 all-reduce.7
  442.8 47.3 all-reduce.11
  495.1 53.6 all-reduce.9
where the time goes:
time: 694 us; the launch traced here: 692 us
  blocking collectives  238 us (34%)
  waiting for transfers between devices  228 us (33%)
  local copies, waits for them, and re-layouts  79.7 us (11%)
  other arithmetic  79.7 us (11%)
  matrix products  33.6 us (5%)
  between operations  18.1 us (3%)
  starting transfers between devices  14.8 us (2%)
    all_gather x2, blocking collectives, gather_rows(): by_expert = lax.all_gather(rows, 'expert', axis=0, tiled=True)  210 us
    all_to_all x1, waiting for transfers between devices, migrate(): lax.all_to_all(out_a, 'expert', split_axis=0, concat_axis=2, tiled=True)  95 us
    unnamed x5, waiting for transfers between devices  86.2 us
    psum x1, waiting for transfers between devices, local(): routed_sum, shared_sum = lax.psum((routed_part, shared_part), 'dp')  46.9 us
    gather x5, local copies, waits for them, and re-layouts, spread_slots(): chosen = jnp.concatenate([gate_up[picks], down[picks][:, None]], axis=1)  25.9 us
    all_gather x2, blocking collectives, gather_rows(): return lax.all_gather(by_expert, 'dp', axis=0, tiled=True)  16.9 us
  transfers between devices with their start and end apart: 6, of which 4 were waited for; matrix products, arithmetic and copies ran while one was open for 16% of the time, Pallas kernels for 0%

commit v1 on v0

--- a/solution.py
+++ b/solution.py
@@ -14,6 +14,12 @@
 ROPE_BASE = 50000.0
 MASKED_SCORE = -1e30
 HIGHEST = lax.Precision.HIGHEST
+
+
+def joined_along(blocks, dim):
+    blocks = jnp.moveaxis(blocks, 0, dim)
+    shape = blocks.shape
+    return blocks.reshape(*shape[:dim], shape[dim] * shape[dim + 1], *shape[dim + 2 :])
 
 
 def rms_plain(values):
@@ -41,7 +47,19 @@
 
 
 def gather_rows(rows):
-    by_expert = lax.all_gather(rows, "expert", axis=0, tiled=True)
+    size = lax.axis_size("expert")
+    pairs = [(i, (i + 1) % size) for i in range(size)]
+    back = [(b, a) for a, b in pairs]
+    lower, upper = ([], [])
+    for lap in range(size - 1):
+        if lap % 2 == 0:
+            lower.append(lax.ppermute(lower[-1] if lower else rows, "expert", pairs))
+        else:
+            upper.append(lax.ppermute(upper[-1] if upper else rows, "expert", back))
+    blocks = jnp.stack([*lower[::-1], rows, *upper])
+    shift = lax.axis_index("expert") - len(lower)
+    blocks = blocks[(jnp.arange(size) - shift) % size]
+    by_expert = joined_along(blocks, 0)
     return lax.all_gather(by_expert, "dp", axis=0, tiled=True)
 
 

time: 694 us -> 673 us (0.970)
  blocking collectives: 238 us -> 28.5 us
  waiting for transfers between devices: 228 us -> 377 us
  starting transfers between devices: 14.8 us -> 72.6 us
  local copies, waits for them, and re-layouts: 79.7 us -> 69.4 us
    all_gather x2 -> x0, blocking collectives: 210 us -> none  [gather_rows(): by_expert = lax.all_gather(rows, 'expert', axis=0, tiled=True)]
    ppermute x0 -> x14, waiting for transfers between devices: none -> 127 us  [the longest x8 124 us: gather_rows(): lower.append(lax.ppermute(lower[-1] if lower else rows, 'expert', pairs))]
    ppermute x0 -> x14, starting transfers between devices: none -> 57.8 us  [the longest x8 36.9 us: gather_rows(): lower.append(lax.ppermute(lower[-1] if lower else rows, 'expert', pairs))]
    unnamed x5, waiting for transfers between devices: 86.2 us -> 109 us
  transfers between devices with their start and end apart: 6 -> 20, of which waited for: 4 -> 11; matrix products, arithmetic and copies ran while one was open for 16% -> 14% of each run, Pallas kernels for 0% -> 0%
where the time goes in v1:
time: 673 us; the launch traced here: 671 us
  waiting for transfers between devices  377 us (56%)
  other arithmetic  73.8 us (11%)
  starting transfers between devices  72.6 us (11%)
  local copies, waits for them, and re-layouts  69.4 us (10%)
  matrix products  31.1 us (5%)
  blocking collectives  28.5 us (4%)
  between operations  18.4 us (3%)
    ppermute x8, waiting for transfers between devices, gather_rows(): lower.append(lax.ppermute(lower[-1] if lower else rows, 'expert', pairs))  124 us
    unnamed x5, waiting for transfers between devices  109 us
    all_to_all x1, waiting for transfers between devices, migrate(): lax.all_to_all(out_a, 'expert', split_axis=0, concat_axis=2, tiled=True)  95 us
    psum x1, waiting for transfers between devices, local(): routed_sum, shared_sum = lax.psum((routed_part, shared_part), 'dp')  46.1 us
    ppermute x8, starting transfers between devices, gather_rows(): lower.append(lax.ppermute(lower[-1] if lower else rows, 'expert', pairs))  36.9 us
    gather x5, local copies, waits for them, and re-layouts, spread_slots(): chosen = jnp.concatenate([gate_up[picks], down[picks][:, None]], axis=1)  25.9 us
    ppermute x6, starting transfers between devices, gather_rows(): upper.append(lax.ppermute(upper[-1] if upper else rows, 'expert', back))  20.8 us
    all_gather x2, blocking collectives, gather_rows(): return lax.all_gather(by_expert, 'dp', axis=0, tiled=True)  16.9 us
  transfers between devices with their start and end apart: 20, of which 11 were waited for; matrix products, arithmetic and copies ran while one was open for 14% of the time, Pallas kernels for 0%

profile of v1, /device:TPU:0, one launch (start us, length us, event | category | flops | bytes accessed | tf_op | source)
XLA Modules:
  0.0 670.7 jit_solution(3587788961913285687)
XLA Ops:
  18.3 5.9 mini-gather-slice.2
  24.2 5.2 mini-gather-slice.3
  30.9 5.2 gather_fusion.13
  36.1 4.7 gather_fusion.14
  40.8 5.0 gather_fusion.10
  45.8 5.6 pad_maximum_fusion.3
  51.4 7.7 %pad_maximum_fusion.2 = bf16[2,3,8,176,512]{4,3,2,1,0:T(8,128)(2,1)} fusion(bf16[2,1,8,176,512]{4,3,2,1,0:T(8,128)(2,1)} %bitcast.240, bf16[2,2,8,176,512]{4,3,2,1,0:T(8,128)(2,1)} %bitcast.236), kind=kLoop, calls=%fused_computation.24 | loop fusion | flops 4325376 | bytes 17301504 | tf_op jit(solution)/shard_map/concatenate | solution.py:67
  59.1 7.6 %copy.166 = bf16[2,3,8,176,512]{4,3,1,0,2:T(8,128)(2,1)} copy(bf16[2,3,8,176,512]{4,3,2,1,0:T(8,128)(2,1)} %pad_maximum_fusion.2) | data formatting | bytes 17301504 | tf_op jit(solution)/shard_map/concatenate | solution.py:67
  71.6 6.5 all-to-all-start.2
  87.3 4.3 compare_select_fusion.5
  92.3 11.1 %select_subtract_fusion = s32[192]{0:T(256)} fusion(pred[192]{0:T(512)(128)(4,1)S(1)} %get-tuple-element.86, pred[192]{0:T(512)(128)(4,1)S(1)} %get-tuple-element.85, pred[192]{0:T(512)(128)(4,1)S(1)} %get-tuple-element.84, pred[192]{0:T(512)(128)(4,1)S(1)} %get-tuple-element.83, pred[192]{0:T(512)(128)(4,1)S(1)} %get-tuple-element.82, ...), kind=kLoop, calls=%fused_computation.217 | loop fusion | flops 3456 | bytes 4872 | tf_op jit(solution)/shard_map/sub | solution.py:271
  104.2 117.7 %collective-permute-done = bf16[1,2048]{1,0:T(2,128)(2,1)S(1)} collective-permute-done((bf16[1,2048]{1,0:T(2,128)(2,1)S(1)}, bf16[1,2048]{1,0:T(2,128)(2,1)S(1)}, u32[]{:S(2)}, u32[]{:S(2)}) %collective-permute-start) | collective-permute-done | bytes 4128 | tf_op jit(solution)/shard_map/ppermute | solution.py:56
  222.0 3.6 collective-permute-start.5
  227.0 3.6 collective-permute-start.6
  231.9 36.4 %collective-permute-start.3 = (bf16[1,2048]{1,0:T(2,128)(2,1)S(1)}, bf16[1,2048]{1,0:T(2,128)(2,1)S(1)}, u32[]{:S(2)}, u32[]{:S(2)}) collective-permute-start(bf16[1,2048]{1,0:T(2,128)(2,1)S(1)} %collective-permute-done.2), channel_id=1, source_target_pairs={{0,1},{1,2},{2,3},{3,4},{4,5},{5,6},{6,7},{7,0},{8,9},{9,10},{10,1... | collective-permute-start | bytes 12296 | tf_op jit(solution)/shard_map/ppermute | solution.py:56
  271.6 8.5 %all-gather = bf16[32,2048]{1,0:T(8,128)(2,1)S(1)} all-gather(bf16[8,2048]{1,0:T(8,128)(2,1)S(1)} %gather_fusion.4), channel_id=2, replica_groups=mesh['dp'=4,'expert'=8] {'dp'}, dimensions={0}, use_global_device_ids=true | all-gather | bytes 163840 | tf_op jit(solution)/shard_map/all_gather | solution.py:63
  297.0 11.6 %all-gather.1 = f32[128,2,514]{2,0,1:T(8,128)S(1)} all-gather(f32[32,2,514]{2,0,1:T(8,128)S(1)} %pad_maximum_fusion.4), channel_id=3, replica_groups=mesh['dp'=4,'expert'=8] {'dp'}, dimensions={0}, use_global_device_ids=true | all-gather | bytes 657920 | tf_op jit(solution)/shard_map/all_gather | solution.py:208
  323.5 55.4 %all-reduce.8.cloned.1.call-done = f32[8,2048]{1,0:T(8,128)} async-done(((f32[8,2048]{1,0:T(8,128)}), f32[8,2048]{1,0:T(8,128)}) %all-reduce.8.cloned.1.call-update) | async-done | bytes 65552
  383.4 3.5 collective-permute-start.11
  398.0 3.5 collective-permute-done.10
  402.3 8.4 %all-gather.2 = bf16[32,2048]{1,0:T(8,128)(2,1)S(1)} all-gather(bf16[8,2048]{1,0:T(8,128)(2,1)S(1)} %gather_fusion.8), channel_id=4, replica_groups=mesh['dp'=4,'expert'=8] {'dp'}, dimensions={0}, use_global_device_ids=true | all-gather | bytes 163840 | tf_op jit(solution)/shard_map/all_gather | solution.py:63
  410.8 4.9 convolution_bitcast_fusion
  415.7 6.9 %convolution_bitcast_fusion.1 = f32[4,2,16,1408]{3,2,1,0:T(8,128)} fusion(bf16[4,2,1408,512]{3,2,1,0:T(8,128)(2,1)} %param.34, bf16[32,512,1]{1,0,2:T(8,128)(2,1)S(1)} %reshape.721, bf16[32,4,16]{0,2,1:T(8,128)(2,1)S(1)} %get-tuple-element.68), kind=kOutput, calls=%fused_computation.30 | convolution fusion | flops 186679296 | bytes 12292096 | tf_op jit(solution)/shard_map/scd,sgfd->sgcf/dot_general | solution.py:284
  423.3 46.1 %all-reduce.12.cloned.1.call-done = (f32[2,4,2816]{2,1,0:T(4,128)}, f32[4,2,16,1408]{3,2,1,0:T(8,128)}) async-done(((f32[2,4,2816]{2,1,0:T(4,128)}, f32[4,2,16,1408]{3,2,1,0:T(8,128)}), (f32[2,4,2816]{2,1,0:T(4,128)}, f32[4,2,16,1408]{3,2,1,0:T(8,128)})) %all-reduce.12.cloned.1.call-update) | async-done | bytes 811024 | tf_op jit(solution)/shard_map/psum | solution.py:290
  469.4 3.8 fusion.18
  474.7 53.1 %all-reduce.10.cloned.1.call-done = f32[32,512]{1,0:T(8,128)} async-done(((f32[32,512]{1,0:T(8,128)}), f32[32,512]{1,0:T(8,128)}) %all-reduce.10.cloned.1.call-update) | async-done | bytes 65552
  529.7 3.6 all-to-all-start.1
  533.3 6.3 gather_fusion.11
  539.7 6.1 broadcast_select_fusion.2
  545.8 4.6 all-to-all-start.3
  552.2 95.0 %all-to-all-done.3 = bf16[8,3,176,512]{3,2,1,0:T(8,128)(2,1)} async-done(((bf16[8,3,176,512]{3,2,1,0:T(8,128)(2,1)}), bf16[8,3,176,512]{3,2,1,0:T(8,128)(2,1)}, u32[]{:S(2)}, u32[]{:S(2)}) %all-to-all-start.3) | async-done | bytes 4325408 | tf_op jit(solution)/shard_map/all_to_all | solution.py:118
  650.0 11.0 %broadcast_select_fusion = bf16[4,2,1408,512]{3,2,1,0:T(8,128)(2,1)} fusion(bf16[4,2,1408,512]{3,2,1,0:T(8,128)(2,1)} %param.34, pred[4]{0:T(512)(128)(4,1)S(1)} %iota_compare_fusion.9, bf16[2,1408,512]{2,1,0:T(8,128)(2,1)S(1)} %slice_bitcast_fusion), kind=kLoop, calls=%fused_computation.23 | loop fusion | flops 5767168 | bytes 25952260 | tf_op jit(solution)/shard_map/jit(_where)/select_n | solution.py:120
  (239 shorter events, 92.6 us)
Async XLA Ops:
  7.2 520.7 %copy-start = (bf16[2816,512]{1,0:T(8,128)(2,1)S(1)}, bf16[2816,512]{1,0:T(8,128)(2,1)}, u32[]{:S(2)}) copy-start(bf16[2816,512]{1,0:T(8,128)(2,1)} %param.37) | copy-start | bytes 8650756
  71.6 20.1 %copy-start.21 = (s32[32]{0:T(128)S(1)}, s32[32]{0:T(128)}, u32[]{:S(2)}) copy-start(s32[32]{0:T(128)} %param.28) | copy-start | bytes 388
  71.6 208.7 %copy-start.12 = (f32[2048]{0:T(1024)S(1)}, f32[2048]{0:T(1024)}, u32[]{:S(2)}) copy-start(f32[2048]{0:T(1024)} %param.21) | copy-start | bytes 24580
  71.6 458.1 %all-to-all-start.2 = ((bf16[2,3,8,176,512]{4,3,1,0,2:T(8,128)(2,1)}), bf16[2,3,8,176,512]{4,3,1,0,2:T(8,128)(2,1)}, u32[]{:S(2)}, u32[]{:S(2)}) async-start(bf16[2,3,8,176,512]{4,3,1,0,2:T(8,128)(2,1)} %copy.166), calls=%async_computation.2 | async-start | bytes 17301504 | tf_op jit(solution)/shard_map/all_to_all | solution.py:70
  78.1 300.8 %all-reduce.8.cloned.1.call-start = ((), (), s32[]{:S(2)}) async-start(), calls=%async_computation.4 | async-start | bytes 131072
  78.1 143.8 %collective-permute-start = (bf16[1,2048]{1,0:T(2,128)(2,1)S(1)}, bf16[1,2048]{1,0:T(2,128)(2,1)S(1)}, u32[]{:S(2)}, u32[]{:S(2)}) collective-permute-start(bf16[1,2048]{1,0:T(2,128)(2,1)S(1)} %copy-done.5), channel_id=1, source_target_pairs={{0,1},{1,2},{2,3},{3,4},{4,5},{5,6},{6,7},{7,0},{8,9},{9,10},{10,1... | collective-permute-start | bytes 12296 | tf_op jit(solution)/shard_map/ppermute | solution.py:56
  78.6 143.3 %collective-permute-start.4 = (bf16[1,2048]{1,0:T(2,128)(2,1)S(1)}, bf16[1,2048]{1,0:T(2,128)(2,1)S(1)}, u32[]{:S(2)}, u32[]{:S(2)}) collective-permute-start(bf16[1,2048]{1,0:T(2,128)(2,1)S(1)} %copy-done.5), channel_id=1, source_target_pairs={{1,0},{2,1},{3,2},{4,3},{5,4},{6,5},{7,6},{0,7},{9,8},{10,9},{11,1... | collective-permute-start | bytes 12296 | tf_op jit(solution)/shard_map/ppermute | solution.py:58
  84.8 186.1 %copy-start.17 = (f32[32]{0:T(128)}, f32[32]{0:T(128)S(1)}, u32[]{:S(2)}) copy-start(f32[32]{0:T(128)S(1)} %multiply_exponential_fusion) | copy-start | bytes 388
  85.4 18.8 %copy-start.10 = (s32[32]{0:T(128)}, s32[32]{0:T(128)S(1)}, u32[]{:S(2)}) copy-start(s32[32]{0:T(128)S(1)} %get-tuple-element.101) | copy-start | bytes 388
  222.0 5.0 collective-permute-start.1
  222.0 5.0 collective-permute-start.5
  226.9 5.0 collective-permute-start.2
  226.9 53.3 %copy-start.14 = (s32[1024]{0:T(1024)}, s32[1024]{0:T(1024)S(1)}, u32[]{:S(2)}) copy-start(s32[1024]{0:T(1024)S(1)} %pad_clamp_fusion.6) | copy-start | bytes 12292
  227.0 43.9 %collective-permute-start.6 = (bf16[1,2048]{1,0:T(2,128)(2,1)S(1)}, bf16[1,2048]{1,0:T(2,128)(2,1)S(1)}, u32[]{:S(2)}, u32[]{:S(2)}) collective-permute-start(bf16[1,2048]{1,0:T(2,128)(2,1)S(1)} %collective-permute-done.5), channel_id=1, source_target_pairs={{1,0},{2,1},{3,2},{4,3},{5,4},{6,5},{7,6},{0,7},{9,8},{10,9},{11,1... | collective-permute-start | bytes 12296 | tf_op jit(solution)/shard_map/ppermute | solution.py:58
  231.9 38.9 %collective-permute-start.3 = (bf16[1,2048]{1,0:T(2,128)(2,1)S(1)}, bf16[1,2048]{1,0:T(2,128)(2,1)S(1)}, u32[]{:S(2)}, u32[]{:S(2)}) collective-permute-start(bf16[1,2048]{1,0:T(2,128)(2,1)S(1)} %collective-permute-done.2), channel_id=1, source_target_pairs={{0,1},{1,2},{2,3},{3,4},{4,5},{5,6},{6,7},{7,0},{8,9},{9,10},{10,1... | collective-permute-start | bytes 12296 | tf_op jit(solution)/shard_map/ppermute | solution.py:56
  270.1 38.5 %copy-start.1 = (bf16[512,512]{0,1:T(8,128)(2,1)}, bf16[512,512]{0,1:T(8,128)(2,1)S(1)}, u32[]{:S(2)}) copy-start(bf16[512,512]{0,1:T(8,128)(2,1)S(1)} %copy.145) | copy-start | bytes 1572868
  312.2 66.7 %copy-start.6 = (bf16[1,2048]{1,0:T(2,128)(2,1)S(1)}, bf16[1,2048]{1,0:T(2,128)(2,1)}, u32[]{:S(2)}) copy-start(bf16[1,2048]{1,0:T(2,128)(2,1)} %param.20) | copy-start | bytes 12292
  312.2 69.5 %copy-start.13 = (f32[2048]{0:T(1024)S(1)}, f32[2048]{0:T(1024)}, u32[]{:S(2)}) copy-start(f32[2048]{0:T(1024)} %param.29) | copy-start | bytes 24580
  312.2 79.8 %copy-start.16 = (f32[32,6]{0,1:T(8,128)S(1)}, f32[32,6]{0,1:T(8,128)}, u32[]{:S(2)}) copy-start(f32[32,6]{0,1:T(8,128)} %param.31) | copy-start | bytes 2308
  322.9 146.5 %all-reduce.12.cloned.1.call-start = ((), (), s32[]{:S(2)}) async-start(), calls=%async_computation.6 | async-start | bytes 1622016 | tf_op jit(solution)/shard_map/psum | solution.py:290
  381.7 5.2 collective-permute-start.7
  383.4 4.9 collective-permute-start.11
  386.9 4.9 collective-permute-start.8
  388.3 4.9 collective-permute-start.12
  391.8 4.9 collective-permute-start.9
  393.1 4.9 collective-permute-start.13
  396.7 4.9 collective-permute-start.10
  422.6 105.2 %all-reduce.10.cloned.1.call-start = ((), (), s32[]{:S(2)}) async-start(), calls=%async_computation.5 | async-start | bytes 131072
  469.4 58.5 %copy-start.8 = (f32[2,4,2816]{2,1,0:T(4,128)S(1)}, f32[2,4,2816]{2,1,0:T(4,128)}, u32[]{:S(2)}) copy-start(f32[2,4,2816]{2,1,0:T(4,128)} %get-tuple-element.87) | copy-start | bytes 270340
  529.7 16.1 %all-to-all-start.1 = ((f32[4,1,512]{2,1,0:T(1,128)}), f32[4,1,512]{2,1,0:T(1,128)S(1)}, u32[]{:S(2)}, u32[]{:S(2)}) async-start(f32[4,1,512]{2,1,0:T(1,128)} %copy.164), calls=%async_computation.1 | async-start | bytes 16384 | tf_op jit(solution)/shard_map/all_to_all | solution.py:299
  545.8 101.4 %all-to-all-start.3 = ((bf16[8,3,176,512]{3,2,1,0:T(8,128)(2,1)}), bf16[8,3,176,512]{3,2,1,0:T(8,128)(2,1)}, u32[]{:S(2)}, u32[]{:S(2)}) async-start(bf16[8,3,176,512]{3,2,1,0:T(8,128)(2,1)} %broadcast_select_fusion.2), calls=%async_computation.3 | async-start | bytes 8650752 | tf_op jit(solution)/shard_map/all_to_all | solution.py:118
  649.7 11.3 %slice-start = ((s8[5767168]{0:T(1024)(128)(4,1)}), s8[4194304]{0:T(1024)(128)(4,1)S(1)}, s32[]{:S(2)}) async-start(s8[5767168]{0:T(1024)(128)(4,1)} %bitcast.234), calls=%async_computation.7 | async-start | bytes 8388608
  (13 other events, 77.5 us)
Sparse Core Ops, SparseCore 0:
  323.0 55.8 all-reduce.7
  422.7 46.5 all-reduce.11
  474.2 53.6 all-reduce.9
